TPU v7x, 256 devices: a whole 4x4x8 slice. The times are simulated.
256 devices in a mesh: row: 32 (over x, z), col: 8 (over y, core).
Axes of the slice: x: 4, y: 4, z: 8, core: 2. Of those that a mesh axis runs over, the one named last changes fastest.
Arguments:
- points: float32 [16384, 256], P('row'), may hold values from -6 to 6
- nugget: float32 [16384], P('row'), may hold values from 0.5 to 2
- weights: float32 [256], replicated, may hold values from 0.0005 to 0.005
- band_start: int32 [32], replicated, may hold values from 0 to 30, as said below
Outputs:
- factored: float32 [32, 4, 8, 512, 512], P('row', None, 'col')
Inputs may be any that keep to these rules, and one draw needn't show every extreme that they name: band_start[i] <= i - 1 for every i >= 1, band_start[0] = 0; band_start[17] = 0; the last tile row has band_start = 30.
All inputs are finite; a program needn't handle non-finite values.
Results may differ from a plain program's by a relative error of at most 0.0003.
Values sent between devices are 32-bit elements; how exact they have to be, the bound alone decides.
No kernel may reach another device: no remote copies, remote signals or barrier semaphores. Data moves between devices by JAX's collectives and lax.ppermute only.
A program may use at most 128 MiB of HBM per device.

v0:
```python
import jax
import jax.numpy as jnp
from jax import lax
from jax.sharding import PartitionSpec as P


def broadcast(value, axis, source):
    kept = jnp.where(lax.axis_index(axis) == source, value, 0).astype(value.dtype)
    return lax.psum(kept, axis)


def kernel_tile(xrow, xcol, weights):
    weighted = xrow * weights
    sq_row = jnp.sum(weighted * xrow, axis=1)
    sq_col = jnp.sum(xcol * xcol * weights, axis=1)
    cross = jnp.dot(
        weighted, xcol.T, precision=lax.Precision.HIGHEST, preferred_element_type=jnp.float32
    )
    dist_sq = jnp.maximum(sq_row[:, None] + sq_col[None, :] - 2.0 * cross, 0.0)
    dist = jnp.sqrt(3.0 * dist_sq)
    return (1.0 + dist) * jnp.exp(-dist)


def factor_panel(local, p, n_col, my_row):
    owner_col = p % n_col
    diag_tile = broadcast(local, "row", p)
    lpp = jnp.linalg.cholesky(diag_tile)
    solved = jax.scipy.linalg.solve_triangular(lpp, local.T, lower=True).T
    panel = broadcast(solved, "col", owner_col)
    panel = jnp.where(my_row > p, panel, jnp.where(my_row == p, lpp, jnp.float32(0.0)))
    return panel


def column_factors(panel, my_col, n_col, blocks):
    width = panel.shape[1]
    slab = panel.shape[0] // (n_col * blocks)
    mixed = lax.all_to_all(panel, "row", split_axis=0, concat_axis=0, tiled=True)
    picked = lax.dynamic_slice_in_dim(mixed.reshape(blocks, n_col, slab, width), my_col, 1, 1)
    picked = picked.reshape(blocks, slab, width)
    whole = lax.all_gather(picked, "row", axis=1, tiled=True)
    return [whole[k] for k in range(blocks)]


def apply_panel(tiles, panel, col_tiles, p, my_row, my_col, n_col):
    result = []
    for k in range(len(tiles)):
        column = my_col + n_col * k
        prod = jnp.dot(
            panel,
            col_tiles[k].T,
            precision=lax.Precision.HIGHEST,
            preferred_element_type=jnp.float32,
        )
        live = (column > p) & (column <= my_row)
        block = tiles[k] - jnp.where(live, prod, jnp.float32(0.0))
        result.append(jnp.where(column == p, panel, block))
    return result


def body(points, nugget, weights, band_start):
    n_row = lax.axis_size("row")
    n_col = lax.axis_size("col")
    blocks = n_row // n_col
    my_row = lax.axis_index("row")
    my_col = lax.axis_index("col")
    diag_nugget = jnp.diag(nugget)
    tiles = []
    for k in range(blocks):
        column = my_col + n_col * k
        xcol = broadcast(points, "row", column)
        block = kernel_tile(points, xcol, weights)
        keep = (column >= band_start[my_row]) & (column <= my_row)
        block = jnp.where(keep, block, jnp.float32(0.0))
        tiles.append(block + jnp.where(column == my_row, diag_nugget, jnp.float32(0.0)))
    for p in range(2):
        panel = factor_panel(tiles[p // n_col], p, n_col, my_row)
        col_tiles = column_factors(panel, my_col, n_col, blocks)
        tiles = apply_panel(tiles, panel, col_tiles, p, my_row, my_col, n_col)
    stacked_tiles = jnp.stack(tiles)
    return stacked_tiles.reshape(1, blocks, 1, points.shape[0], points.shape[0])


def solution(mesh):
    placed = (P("row", None), P("row"), P(), P())
    return jax.shard_map(
        body,
        mesh=mesh,
        in_specs=placed,
        out_specs=P("row", None, "col", None, None),
        check_vma=False,
    )
```

profile of v0, /device:TPU:8, one launch (start us, length us, event | category | flops | bytes accessed | tf_op | source)
XLA Modules:
  0.0 1198.2 jit_solution(10139373326444151370)
XLA Ops:
  10.4 158.8 %all-reduce.16.cloned.1.call-done = (f32[512,256]{1,0:T(8,128)}, f32[512,256]{1,0:T(8,128)}, f32[512,256]{1,0:T(8,128)}, f32[512,256]{1,0:T(8,128)}) async-done(((f32[512,256]{1,0:T(8,128)}, f32[512,256]{1,0:T(8,128)}, f32[512,256]{1,0:T(8,128)}, f32[512,256]{1,0:T(8,128)}), (f32[512,256]{1,0:T(8,128)}, f32[512,256]{1,0:T(8,128)}, f32[512,256]{1,0:T(8,128)}, ...) | async-done | bytes 2097168 | tf_op jit(solution)/shard_map/psum | solution.py:9
  178.3 147.6 %all-reduce.8.cloned.1.call-done = f32[512,512]{0,1:T(8,128)} async-done(((f32[512,512]{0,1:T(8,128)}), f32[512,512]{0,1:T(8,128)}) %all-reduce.8.cloned.1.call-update) | async-done | bytes 1048592 | tf_op jit(solution)/shard_map/psum | solution.py:9
  329.9 11.7 cholesky.286
  354.2 11.7 cholesky.305
  366.1 10.0 custom-call.28
  378.1 11.7 cholesky.326
  401.4 12.1 %cholesky.343 = f32[128,128]{1,0:T(8,128)S(1)} custom-call(f32[128,128]{1,0:T(8,128)S(1)} %convolution_subtract_fusion.11), custom_call_target="Cholesky" | custom-call | tf_op jit(solution)/shard_map/jit(cholesky)/cholesky | solution.py:27
  419.3 12.3 %while.4 = (s32[]{:T(128)}, f32[512,512]{0,1:T(8,128)}, s32[4,2]{0,1:T(2,128)S(1)}, f32[4,128,128]{2,1,0:T(8,128)S(1)}, s32[]{:T(128)}) while((s32[]{:T(128)}, f32[512,512]{0,1:T(8,128)}, s32[4,2]{0,1:T(2,128)S(1)}, f32[4,128,128]{2,1,0:T(8,128)S(1)}, s32[]{:T(128)}) %tuple.57), condition=%wide.while_cond, body=%wide.while_body.sunk | while | flops 2 | bytes 393329 | solution.py:28
  431.6 39.3 %custom-call.30 = f32[4,128,128]{1,2,0:T(8,128)S(1)} custom-call(f32[4,128,128]{2,1,0:T(8,128)S(1)} %get-tuple-element.21), custom_call_target="InvertDiagBlocksLowerTriangular" | custom-call | tf_op jit(solution)/shard_map/jit(_solve_triangular)/triangular_solve | solution.py:28
  486.3 62.9 %all-reduce.10.cloned.1.call-done = f32[512,512]{1,0:T(8,128)} async-done(((f32[512,512]{1,0:T(8,128)}), f32[512,512]{1,0:T(8,128)}) %all-reduce.10.cloned.1.call-update) | async-done | bytes 1048592 | tf_op jit(solution)/shard_map/psum | solution.py:9
  555.4 11.0 all-to-all-start
  566.5 26.7 %all-to-all-done = f32[32,16,512]{2,1,0:T(8,128)S(1)} async-done(((f32[32,16,512]{2,1,0:T(8,128)}), f32[32,16,512]{2,1,0:T(8,128)S(1)}, u32[]{:S(2)}, u32[]{:S(2)}) %all-to-all-start) | async-done | bytes 1048608 | tf_op jit(solution)/shard_map/all_to_all | solution.py:37
  593.9 81.1 %all-gather.5.cloned.1.call-done = f32[4,1,512,512]{3,2,1,0:T(8,128)} async-done(((f32[4,1,16,512]{3,2,1,0:T(8,128)}), f32[4,1,512,512]{3,2,1,0:T(8,128)}) %all-gather.5.cloned.1.call-update) | async-done | bytes 4194320 | tf_op jit(solution)/shard_map/all_gather | solution.py:40
  680.7 147.2 %all-reduce.12.cloned.1.call-done = f32[512,512]{0,1:T(8,128)} async-done(((f32[512,512]{0,1:T(8,128)}), f32[512,512]{0,1:T(8,128)}) %all-reduce.12.cloned.1.call-update) | async-done | bytes 1048592 | tf_op jit(solution)/shard_map/psum | solution.py:9
  831.9 11.7 cholesky.358
  856.2 11.7 cholesky.377
  868.1 10.0 custom-call.32
  880.1 11.7 cholesky.398
  903.4 12.1 %cholesky.415 = f32[128,128]{1,0:T(8,128)S(1)} custom-call(f32[128,128]{1,0:T(8,128)S(1)} %convolution_subtract_fusion.10), custom_call_target="Cholesky" | custom-call | tf_op jit(solution)/shard_map/jit(cholesky)/cholesky | solution.py:27
  921.9 12.3 %while.5 = (s32[]{:T(128)}, f32[512,512]{0,1:T(8,128)}, s32[4,2]{0,1:T(2,128)S(1)}, f32[4,128,128]{2,1,0:T(8,128)S(1)}, s32[]{:T(128)}) while((s32[]{:T(128)}, f32[512,512]{0,1:T(8,128)}, s32[4,2]{0,1:T(2,128)S(1)}, f32[4,128,128]{2,1,0:T(8,128)S(1)}, s32[]{:T(128)}) %tuple.78), condition=%wide.while_cond.clone, body=%wide.while_body.clone.sunk | while | flops 2 | bytes 393329 | solution.py:28
  934.2 39.3 %custom-call.34 = f32[4,128,128]{1,2,0:T(8,128)S(1)} custom-call(f32[4,128,128]{2,1,0:T(8,128)S(1)} %get-tuple-element.22), custom_call_target="InvertDiagBlocksLowerTriangular" | custom-call | tf_op jit(solution)/shard_map/jit(_solve_triangular)/triangular_solve | solution.py:28
  986.2 62.8 %all-reduce.14.cloned.1.call-done = f32[512,512]{1,0:T(8,128)} async-done(((f32[512,512]{1,0:T(8,128)}), f32[512,512]{1,0:T(8,128)}) %all-reduce.14.cloned.1.call-update) | async-done | bytes 1048592 | tf_op jit(solution)/shard_map/psum | solution.py:9
  1053.1 38.0 %all_to_all.18 = f32[32,16,512]{2,1,0:T(8,128)S(1)} all-to-all(f32[32,16,512]{2,1,0:T(8,128)} %bitcast.160), channel_id=1, replica_groups=mesh['row'=32,'col'=8] {'row'}, dimensions={0} | all-to-all | bytes 2097152 | tf_op jit(solution)/shard_map/all_to_all | solution.py:37
  1109.6 63.2 %all-gather.7.cloned.1.call-done = f32[4,1,512,512]{3,2,1,0:T(8,128)} async-done(((f32[4,1,16,512]{3,2,1,0:T(8,128)}), f32[4,1,512,512]{3,2,1,0:T(8,128)}) %all-gather.7.cloned.1.call-update) | async-done | bytes 4194320 | tf_op jit(solution)/shard_map/all_gather | solution.py:40
  (204 shorter events, 183.6 us)
Async XLA Ops:
  6.5 162.6 %copy-start = (f32[512,256]{1,0:T(8,128)S(1)}, f32[512,256]{1,0:T(8,128)}, u32[]{:S(2)}) copy-start(f32[512,256]{1,0:T(8,128)} %param.7) | copy-start | bytes 1572868
  6.5 2.6 copy-start.16
  6.5 162.6 %copy-start.13 = (f32[256]{0:T(256)S(1)}, f32[256]{0:T(256)}, u32[]{:S(2)}) copy-start(f32[256]{0:T(256)} %param.9) | copy-start | bytes 3076
  6.5 162.6 %all-reduce.16.cloned.1.call-start = ((), (), s32[]{:S(2)}) async-start(), calls=%async_computation.8 | async-start | bytes 4194304 | tf_op jit(solution)/shard_map/psum | solution.py:9
  9.0 166.8 %copy-start.14 = (f32[512]{0:T(512)S(1)}, f32[512]{0:T(512)}, u32[]{:S(2)}) copy-start(f32[512]{0:T(512)} %param.8) | copy-start | bytes 6148
  9.1 316.8 %all-reduce.8.cloned.1.call-start = ((), (), s32[]{:S(2)}) async-start(), calls=%async_computation.2 | async-start | bytes 2097152 | tf_op jit(solution)/shard_map/psum | solution.py:9
  178.1 371.0 %all-reduce.10.cloned.1.call-start = ((), (), s32[]{:S(2)}) async-start(), calls=%async_computation.3 | async-start | bytes 2097152 | tf_op jit(solution)/shard_map/psum | solution.py:9
  471.0 5.2 copy-start.11
  555.4 37.8 %all-to-all-start = ((f32[32,16,512]{2,1,0:T(8,128)}), f32[32,16,512]{2,1,0:T(8,128)S(1)}, u32[]{:S(2)}, u32[]{:S(2)}) async-start(f32[32,16,512]{2,1,0:T(8,128)} %bitcast.14), calls=%async_computation | async-start | bytes 2097152 | tf_op jit(solution)/shard_map/all_to_all | solution.py:37
  566.4 108.6 %all-gather.5.cloned.1.call-start = ((), (), s32[]{:S(2)}) async-start(), calls=%async_computation.6 | async-start | bytes 4325376 | tf_op jit(solution)/shard_map/all_gather | solution.py:40
  593.9 234.0 %all-reduce.12.cloned.1.call-start = ((), (), s32[]{:S(2)}) async-start(), calls=%async_computation.4 | async-start | bytes 2097152 | tf_op jit(solution)/shard_map/psum | solution.py:9
  680.4 299.6 %copy-start.2 = (f32[512,512]{0,1:T(8,128)}, f32[512,512]{0,1:T(8,128)S(1)}, u32[]{:S(2)}) copy-start(f32[512,512]{0,1:T(8,128)S(1)} %get-tuple-element.89) | copy-start | bytes 3145732
  680.5 368.5 %all-reduce.14.cloned.1.call-start = ((), (), s32[]{:S(2)}) async-start(), calls=%async_computation.5 | async-start | bytes 2097152 | tf_op jit(solution)/shard_map/psum | solution.py:9
  830.9 1.0 copy-start.7
  973.5 3.8 copy-start.12
  986.1 186.7 %all-gather.7.cloned.1.call-start = ((), (), s32[]{:S(2)}) async-start(), calls=%async_computation.7 | async-start | bytes 4325376 | tf_op jit(solution)/shard_map/all_gather | solution.py:40
  1051.7 47.1 %copy-start.8 = (f32[512,256]{1,0:T(8,128)S(1)}, f32[512,256]{1,0:T(8,128)}, u32[]{:S(2)}) copy-start(f32[512,256]{1,0:T(8,128)} %get-tuple-element.63) | copy-start | bytes 1572868
  1053.1 47.2 %copy-start.4 = (f32[512,512]{0,1:T(8,128)S(1)}, f32[512,512]{0,1:T(8,128)}, u32[]{:S(2)}) copy-start(f32[512,512]{0,1:T(8,128)} %select_select_fusion.5) | copy-start | bytes 3145732
  1093.6 6.7 copy-start.15
  1096.2 7.1 copy-start.5
  1103.3 69.5 %copy-start.3 = (f32[512,512]{0,1:T(8,128)S(1)}, f32[512,512]{0,1:T(8,128)}, u32[]{:S(2)}) copy-start(f32[512,512]{0,1:T(8,128)} %copy-done.2) | copy-start | bytes 3145732
  1172.8 3.3 copy-start.1
  1172.8 6.7 copy-start.9
  1176.1 5.5 copy-start.10
  (1 other events, 1.0 us)
Sparse Core Ops, SparseCore 0:
  11.2 157.8 all-reduce.15
  178.2 147.6 all-reduce.7
  486.4 62.7 all-reduce.9
  594.0 80.9 all-gather.4
  680.6 147.2 all-reduce.11
  986.3 62.7 all-reduce.13
  1091.8 80.9 all-gather.6
where the time goes:
time: 1200 us
  waiting for transfers between devices  750 us (62%)
  other arithmetic  257 us (21%)
  matrix products  67 us (6%)
  local copies, waits for them, and re-layouts  52.1 us (4%)
  blocking collectives  38 us (3%)
  between operations  22.1 us (2%)
    psum x5, waiting for transfers between devices, broadcast(): return lax.psum(kept, axis)  579 us
    another operation x29, other arithmetic, factor_panel(): lpp = jnp.linalg.cholesky(diag_tile)  159 us
    all_gather x2, waiting for transfers between devices, column_factors(): whole = lax.all_gather(picked, 'row', axis=1, tiled=True)  144 us
    another operation x5, other arithmetic, factor_panel(): solved = jax.scipy.linalg.solve_triangular(lpp, local.T, lower=True).T  80.8 us
    all_to_all x1, blocking collectives, column_factors(): lax.all_to_all(panel, 'row', split_axis=0, concat_axis=0, tiled=True)  38 us
    another operation x49, local copies, waits for them, and re-layouts, factor_panel(): solved = jax.scipy.linalg.solve_triangular(lpp, local.T, lower=True).T  28 us
    all_to_all x1, waiting for transfers between devices, column_factors(): lax.all_to_all(panel, 'row', split_axis=0, concat_axis=0, tiled=True)  26.7 us
    dot_general x8, matrix products, apply_panel(): jnp.dot(panel, col_tiles[k].T, precision=lax.Precision.HIGHEST, preferred...  25.5 us
  transfers between devices with their start and end apart: 8, of which 8 were waited for; matrix products, arithmetic and copies ran while one was open for 1% of the time, Pallas kernels for 0%

commit v1 on v0

--- a/solution.py
+++ b/solution.py
@@ -6,7 +6,7 @@
 
 def broadcast(value, axis, source):
     kept = jnp.where(lax.axis_index(axis) == source, value, 0).astype(value.dtype)
-    return lax.psum(kept, axis)
+    return jnp.sum(lax.all_gather(kept, axis), axis=0)
 
 
 def kernel_tile(xrow, xcol, weights):

time: 1200 us -> 1770 us (1.48)
  waiting for transfers between devices: 750 us -> 1260 us
  other arithmetic: 257 us -> 316 us
    all_gather x0 -> x8, waiting for transfers between devices: none -> 1090 us  [broadcast(): return jnp.sum(lax.all_gather(kept, axis), axis=0)]
    psum x5 -> x0, waiting for transfers between devices: 579 us -> none  [broadcast(): return lax.psum(kept, axis)]
    reduce_sum x0 -> x8, other arithmetic: none -> 58.8 us  [broadcast(): return jnp.sum(lax.all_gather(kept, axis), axis=0)]
    unnamed x34 -> x42, local copies, waits for them, and re-layouts: 2 us -> 26.4 us
  transfers between devices with their start and end apart: 8 -> 11, of which waited for: 8 -> 11; matrix products, arithmetic and copies ran while one was open for 1% -> 2% of each run, Pallas kernels for 0% -> 0%
where the time goes in v1:
time: 1770 us
  waiting for transfers between devices  1260 us (71%)
  other arithmetic  316 us (18%)
  matrix products  61 us (3%)
  local copies, waits for them, and re-layouts  57.3 us (3%)
  blocking collectives  40 us (2%)
  between operations  22.1 us (1%)
    all_gather x8, waiting for transfers between devices, broadcast(): return jnp.sum(lax.all_gather(kept, axis), axis=0)  1090 us
    another operation x29, other arithmetic, factor_panel(): lpp = jnp.linalg.cholesky(diag_tile)  158 us
    all_gather x2, waiting for transfers between devices, column_factors(): whole = lax.all_gather(picked, 'row', axis=1, tiled=True)  135 us
    another operation x5, other arithmetic, factor_panel(): solved = jax.scipy.linalg.solve_triangular(lpp, local.T, lower=True).T  83 us
    reduce_sum x8, other arithmetic, broadcast(): return jnp.sum(lax.all_gather(kept, axis), axis=0)  58.8 us
    all_to_all x1, blocking collectives, column_factors(): lax.all_to_all(panel, 'row', split_axis=0, concat_axis=0, tiled=True)  40 us
  transfers between devices with their start and end apart: 11, of which 11 were waited for; matrix products, arithmetic and copies ran while one was open for 2% of the time, Pallas kernels for 0%

profile of v1, /device:TPU:8, one launch (start us, length us, event | category | flops | bytes accessed | tf_op | source)
XLA Modules:
  0.0 1765.6 jit_solution(14467153588467023790)
XLA Ops:
  12.4 140.1 %all-gather.21.cloned.1.call-done = f32[16384,256]{1,0:T(8,128)} async-done(((f32[512,256]{1,0:T(8,128)}), f32[16384,256]{1,0:T(8,128)}) %all-gather.21.cloned.1.call-update) | async-done | bytes 16777232 | tf_op jit(solution)/shard_map/all_gather | solution.py:9
  161.8 130.0 %all-gather.39.cloned.1.call-done = f32[16384,256]{1,0:T(8,128)} async-done(((f32[512,256]{1,0:T(8,128)}), f32[16384,256]{1,0:T(8,128)}) %all-gather.39.cloned.1.call-update) | async-done | bytes 16777232 | tf_op jit(solution)/shard_map/all_gather | solution.py:9
  298.8 132.5 %all-gather.35.cloned.1.call-done = f32[16384,256]{1,0:T(8,128)} async-done(((f32[512,256]{1,0:T(8,128)}), f32[16384,256]{1,0:T(8,128)}) %all-gather.35.cloned.1.call-update) | async-done | bytes 16777232 | tf_op jit(solution)/shard_map/all_gather | solution.py:9
  438.1 132.3 %all-gather.37.cloned.1.call-done = f32[16384,256]{1,0:T(8,128)} async-done(((f32[512,256]{1,0:T(8,128)}), f32[16384,256]{1,0:T(8,128)}) %all-gather.37.cloned.1.call-update) | async-done | bytes 16777232 | tf_op jit(solution)/shard_map/all_gather | solution.py:9
  583.0 230.1 %all-gather.23.cloned.1.call-done = f32[16384,512]{1,0:T(8,128)} async-done(((f32[512,512]{1,0:T(8,128)}), f32[16384,512]{1,0:T(8,128)}) %all-gather.23.cloned.1.call-update) | async-done | bytes 33554448 | tf_op jit(solution)/shard_map/all_gather | solution.py:9
  813.1 12.4 reduce_sum.132
  829.3 11.7 cholesky.286
  853.6 11.7 cholesky.305
  877.1 11.7 cholesky.326
  900.7 11.7 cholesky.343
  929.5 40.1 %custom-call.30 = f32[4,128,128]{1,2,0:T(8,128)S(1)} custom-call(f32[4,128,128]{2,1,0:T(8,128)} %copy-done.15), custom_call_target="InvertDiagBlocksLowerTriangular" | custom-call | tf_op jit(solution)/shard_map/jit(_solve_triangular)/triangular_solve | solution.py:28
  977.0 48.7 %all-gather.25.cloned.1.call-done = f32[4096,512]{0,1:T(8,128)} async-done(((f32[512,512]{0,1:T(8,128)}), f32[4096,512]{0,1:T(8,128)}) %all-gather.25.cloned.1.call-update) | async-done | bytes 8388624 | tf_op jit(solution)/shard_map/all_gather | solution.py:9
  1054.2 29.0 %all-to-all-done = f32[32,16,512]{2,1,0:T(8,128)S(1)} async-done(((f32[32,16,512]{2,1,0:T(8,128)}), f32[32,16,512]{2,1,0:T(8,128)S(1)}, u32[]{:S(2)}, u32[]{:S(2)}) %all-to-all-start) | async-done | bytes 1048608 | tf_op jit(solution)/shard_map/all_to_all | solution.py:37
  1083.9 78.1 %all-gather.27.cloned.1.call-done = f32[4,1,512,512]{3,2,1,0:T(8,128)} async-done(((f32[4,1,16,512]{3,2,1,0:T(8,128)}), f32[4,1,512,512]{3,2,1,0:T(8,128)}) %all-gather.27.cloned.1.call-update) | async-done | bytes 4194320 | tf_op jit(solution)/shard_map/all_gather | solution.py:40
  1167.8 229.8 %all-gather.29.cloned.1.call-done = f32[16384,512]{1,0:T(8,128)} async-done(((f32[512,512]{1,0:T(8,128)}), f32[16384,512]{1,0:T(8,128)}) %all-gather.29.cloned.1.call-update) | async-done | bytes 33554448 | tf_op jit(solution)/shard_map/all_gather | solution.py:9
  1397.6 12.3 reduce_sum.134
  1411.5 11.7 cholesky.358
  1436.3 11.7 cholesky.377
  1460.3 11.7 cholesky.398
  1500.5 11.9 while.5
  1513.1 40.1 %custom-call.34 = f32[4,128,128]{1,2,0:T(8,128)S(1)} custom-call(f32[4,128,128]{2,1,0:T(8,128)} %copy-done.14), custom_call_target="InvertDiagBlocksLowerTriangular" | custom-call | tf_op jit(solution)/shard_map/jit(_solve_triangular)/triangular_solve | solution.py:28
  1561.9 48.6 %all-gather.31.cloned.1.call-done = f32[4096,512]{0,1:T(8,128)} async-done(((f32[512,512]{0,1:T(8,128)}), f32[4096,512]{0,1:T(8,128)}) %all-gather.31.cloned.1.call-update) | async-done | bytes 8388624 | tf_op jit(solution)/shard_map/all_gather | solution.py:9
  1626.6 40.0 %all_to_all.18 = f32[32,16,512]{2,1,0:T(8,128)S(1)} all-to-all(f32[32,16,512]{2,1,0:T(8,128)S(1)} %bitcast.182), channel_id=1, replica_groups=mesh['row'=32,'col'=8] {'row'}, dimensions={0} | all-to-all | bytes 2097152 | tf_op jit(solution)/shard_map/all_to_all | solution.py:37
  1688.5 57.0 %all-gather.33.cloned.1.call-done = f32[4,1,512,512]{3,2,1,0:T(8,128)} async-done(((f32[4,1,16,512]{3,2,1,0:T(8,128)}), f32[4,1,512,512]{3,2,1,0:T(8,128)}) %all-gather.33.cloned.1.call-update) | async-done | bytes 4194320 | tf_op jit(solution)/shard_map/all_gather | solution.py:40
  (186 shorter events, 271.7 us)
Async XLA Ops:
  6.5 145.9 %all-gather.21.cloned.1.call-start = ((), (), s32[]{:S(2)}) async-start(), calls=%async_computation.2 | async-start | bytes 17301504 | tf_op jit(solution)/shard_map/all_gather | solution.py:9
  9.0 282.9 %all-gather.39.cloned.1.call-start = ((), (), s32[]{:S(2)}) async-start(), calls=%async_computation.11 | async-start | bytes 17301504 | tf_op jit(solution)/shard_map/all_gather | solution.py:9
  9.7 421.5 %all-gather.35.cloned.1.call-start = ((), (), s32[]{:S(2)}) async-start(), calls=%async_computation.9 | async-start | bytes 17301504 | tf_op jit(solution)/shard_map/all_gather | solution.py:9
  10.4 560.0 %all-gather.37.cloned.1.call-start = ((), (), s32[]{:S(2)}) async-start(), calls=%async_computation.10 | async-start | bytes 17301504 | tf_op jit(solution)/shard_map/all_gather | solution.py:9
  11.0 802.1 %all-gather.23.cloned.1.call-start = ((), (), s32[]{:S(2)}) async-start(), calls=%async_computation.3 | async-start | bytes 34603008 | tf_op jit(solution)/shard_map/all_gather | solution.py:9
  152.5 6.9 copy-start
  152.5 7.0 copy-start.16
  159.5 139.3 %copy-start.4 = (f32[512,256]{1,0:T(8,128)}, f32[512,256]{1,0:T(8,128)S(1)}, u32[]{:S(2)}) copy-start(f32[512,256]{1,0:T(8,128)S(1)} %reduce_sum.130) | copy-start | bytes 1572868
  438.1 139.2 %copy-start.1 = (f32[512,256]{1,0:T(8,128)}, f32[512,256]{1,0:T(8,128)S(1)}, u32[]{:S(2)}) copy-start(f32[512,256]{1,0:T(8,128)S(1)} %reduce_sum.136) | copy-start | bytes 1572868
  570.5 8.6 copy-start.17
  577.4 248.2 %copy-start.2 = (f32[512,256]{1,0:T(8,128)}, f32[512,256]{1,0:T(8,128)S(1)}, u32[]{:S(2)}) copy-start(f32[512,256]{1,0:T(8,128)S(1)} %reduce_sum.138) | copy-start | bytes 1572868
  583.0 442.7 %all-gather.25.cloned.1.call-start = ((), (), s32[]{:S(2)}) async-start(), calls=%async_computation.4 | async-start | bytes 9437184 | tf_op jit(solution)/shard_map/all_gather | solution.py:9
  829.3 140.3 %copy-start.9 = (f32[512,512]{1,0:T(8,128)S(1)}, f32[512,512]{1,0:T(8,128)}, u32[]{:S(2)}) copy-start(f32[512,512]{1,0:T(8,128)} %get-tuple-element.73) | copy-start | bytes 3145732
  1041.9 120.2 %copy-start.8 = (f32[512,512]{1,0:T(8,128)S(1)}, f32[512,512]{1,0:T(8,128)}, u32[]{:S(2)}) copy-start(f32[512,512]{1,0:T(8,128)} %copy.13) | copy-start | bytes 3145732
  1043.0 40.1 %all-to-all-start = ((f32[32,16,512]{2,1,0:T(8,128)}), f32[32,16,512]{2,1,0:T(8,128)S(1)}, u32[]{:S(2)}, u32[]{:S(2)}) async-start(f32[32,16,512]{2,1,0:T(8,128)} %bitcast.16), calls=%async_computation | async-start | bytes 2097152 | tf_op jit(solution)/shard_map/all_to_all | solution.py:37
  1054.2 107.9 %all-gather.27.cloned.1.call-start = ((), (), s32[]{:S(2)}) async-start(), calls=%async_computation.5 | async-start | bytes 4325376 | tf_op jit(solution)/shard_map/all_gather | solution.py:40
  1083.9 313.8 %all-gather.29.cloned.1.call-start = ((), (), s32[]{:S(2)}) async-start(), calls=%async_computation.6 | async-start | bytes 34603008 | tf_op jit(solution)/shard_map/all_gather | solution.py:9
  1167.8 442.7 %all-gather.31.cloned.1.call-start = ((), (), s32[]{:S(2)}) async-start(), calls=%async_computation.7 | async-start | bytes 9437184 | tf_op jit(solution)/shard_map/all_gather | solution.py:9
  1411.4 141.8 %copy-start.6 = (f32[512,512]{1,0:T(8,128)S(1)}, f32[512,512]{1,0:T(8,128)}, u32[]{:S(2)}) copy-start(f32[512,512]{1,0:T(8,128)} %get-tuple-element.77) | copy-start | bytes 3145732
  1561.9 183.5 %all-gather.33.cloned.1.call-start = ((), (), s32[]{:S(2)}) async-start(), calls=%async_computation.8 | async-start | bytes 4325376 | tf_op jit(solution)/shard_map/all_gather | solution.py:40
  1626.6 45.2 %copy-start.3 = (f32[512,256]{1,0:T(8,128)S(1)}, f32[512,256]{1,0:T(8,128)}, u32[]{:S(2)}) copy-start(f32[512,256]{1,0:T(8,128)} %copy-done.2) | copy-start | bytes 1572868
  1669.2 5.4 copy-start.18
  1679.2 66.2 %copy-start.7 = (f32[512,512]{1,0:T(8,128)S(1)}, f32[512,512]{1,0:T(8,128)}, u32[]{:S(2)}) copy-start(f32[512,512]{1,0:T(8,128)} %get-tuple-element.77) | copy-start | bytes 3145732
  1745.4 6.7 copy-start.12
  (7 other events, 16.6 us)
Sparse Core Ops, SparseCore 0:
  9.9 142.5 all-gather.20
  155.1 136.7 all-gather.38
  294.5 136.7 all-gather.34
  433.7 136.7 all-gather.36
  583.1 229.9 all-gather.22
  977.1 48.5 all-gather.24
  1084.0 77.9 all-gather.26
  1167.9 229.6 all-gather.28
  1562.0 48.4 all-gather.30
  1667.4 77.9 all-gather.32
